TPU v7x, 512 devices: a whole 4x8x8 slice. The times are simulated.
512 devices in a mesh: ctx: 64 (over y, x, core), head: 8 (over z).
Axes of the slice: x: 4, y: 8, z: 8, core: 2. Of those that a mesh axis runs over, the one named last changes fastest.
Arguments:
- tokens: bfloat16 [65536, 2048], P('ctx', 'head'), may hold values from -6 to 6
- w_qkv: bfloat16 [3, 2048, 2048], P(None, 'ctx', 'head'), may hold values from -0.125 to 0.125
- out_gain: float32 [2048], P('head'), may hold values from 0.25 to 1.75
- seg_ids: int32 [65536], P('ctx'), may hold values from 0 to 15, never falling along the last dimension, each value on 1 to 16384 neighbouring positions
Outputs:
- attended: bfloat16 [65536, 2048], P('ctx', 'head')
Inputs may be any that keep to these rules, and one draw needn't show every extreme that they name: `seg_ids`: segment numbers never fall along the stream; each segment covers 1 to 16384 consecutive tokens, and one covers exactly 16384.
All inputs are finite; a program needn't handle non-finite values.
Results may differ from a plain program's by a relative error of at most 0.012.
Values may be sent and summed in bfloat16 or wider, within the bound.
No kernel may reach another device: no remote copies, remote signals or barrier semaphores. Data moves between devices by JAX's collectives and lax.ppermute only.
A program may use at most 64 MiB of HBM per device.

v0:
```python
import jax
import jax.numpy as jnp
from jax import lax
from jax.sharding import PartitionSpec as P

HEAD_DIM = 128
SPAN = 16384


def shifted(value, axis, steps):
    count = lax.axis_size(axis)
    return lax.ppermute(value, axis, [(source, source + steps) for source in range(count - steps)])


def feature_map(values):
    return (jax.nn.elu(values.astype(jnp.float32)) + 1.0).astype(jnp.bfloat16)


def state_scan(kv_state, tail_id, row_count):
    head_count = kv_state.shape[0]
    flat = kv_state.reshape(head_count * HEAD_DIM, HEAD_DIM)
    tail_rows = jnp.full((8, HEAD_DIM), tail_id, jnp.float32)
    packed = jnp.concatenate([flat, tail_rows], axis=0)
    state_rows = head_count * HEAD_DIM
    is_state = (jnp.arange(packed.shape[0]) < state_rows)[:, None]
    count = lax.axis_size("ctx")
    window = min(count - 1, 1 + (SPAN - 1) // row_count)
    running = shifted(packed, "ctx", 1)
    step = 1
    while step < window:
        incoming = shifted(running, "ctx", step)
        linked = incoming[state_rows, 0] == running[state_rows, 0]
        running = running + jnp.where(is_state & linked, incoming, 0.0)
        step *= 2
    state_in = running[:state_rows].reshape(head_count, HEAD_DIM, HEAD_DIM)
    return (state_in, running[state_rows, 0])


def per_device(tokens, w_qkv, out_gain, seg_ids):
    whole = lax.all_gather(tokens, "head", axis=1, tiled=True)
    projected = jnp.einsum(
        "tr,grc->gtc",
        whole,
        lax.all_gather(w_qkv, "ctx", axis=1, tiled=True),
        preferred_element_type=jnp.float32,
    ).astype(jnp.bfloat16)
    row_count = seg_ids.shape[0]
    head_count = projected.shape[2] // HEAD_DIM
    queries = feature_map(projected[0]).reshape(row_count, head_count, HEAD_DIM)
    key_map = feature_map(projected[1]).reshape(row_count, head_count, HEAD_DIM)
    values = projected[2].reshape(row_count, head_count, HEAD_DIM)
    seg_float = seg_ids.astype(jnp.float32)
    tail_id = seg_float[-1]
    key_tail = jnp.where((seg_float == tail_id)[:, None, None], key_map, jnp.zeros_like(key_map))
    kv_state = jnp.einsum("thd,the->hde", key_tail, values, preferred_element_type=jnp.float32)
    state_in, tail_in = state_scan(kv_state, tail_id, row_count)
    block_rows = min(512, row_count)
    pieces = []
    for blk_no in range(row_count // block_rows):
        first_row = blk_no * block_rows
        key_end = first_row + block_rows
        query_blk = queries[first_row:key_end]
        query_pos = first_row + jnp.arange(block_rows, dtype=jnp.int32)
        query_seg = seg_float[first_row:key_end]
        scores = jnp.einsum(
            "bhd,shd->hbs", query_blk, key_map[:key_end], preferred_element_type=jnp.float32
        )
        visible = (jnp.arange(key_end, dtype=jnp.int32)[None, :] <= query_pos[:, None]) & (
            seg_float[None, :key_end] == query_seg[:, None]
        )
        weights = jnp.where(visible[None], scores, 0.0).astype(jnp.bfloat16)
        pieces.append(
            jnp.einsum(
                "hbs,she->bhe", weights, values[:key_end], preferred_element_type=jnp.float32
            )
        )
    local_part = jnp.concatenate(pieces, axis=0)
    state_low = state_in.astype(jnp.bfloat16)
    prefix = jnp.einsum("thd,hde->the", queries, state_low, preferred_element_type=jnp.float32)
    prefix = jnp.where((seg_float == tail_in)[:, None, None], prefix, 0.0)
    numerator = local_part + prefix
    inv_norm = lax.rsqrt(jnp.mean(numerator * numerator, axis=-1, keepdims=True) + 1e-05)
    result = numerator * inv_norm * out_gain.reshape(head_count, HEAD_DIM)
    return result.astype(jnp.bfloat16).reshape(row_count, head_count * HEAD_DIM)


def solution(mesh):
    placed = (P("ctx", "head"), P(None, "ctx", "head"), P("head"), P("ctx"))
    return jax.shard_map(
        per_device, mesh=mesh, in_specs=placed, out_specs=P("ctx", "head"), check_vma=False
    )
```

profile of v0, /device:TPU:32, one launch (start us, length us, event | category | flops | bytes accessed | tf_op | source)
XLA Modules:
  0.0 244.8 jit_solution(2544516807584703272)
XLA Ops:
  9.3 1.3 broadcast_compare_fusion.1
  10.9 1.3 fusion.2
  12.2 84.3 %all-gather.3.cloned.1.call-done = bf16[3,2048,256]{2,1,0:T(8,128)(2,1)} async-done(((bf16[3,32,256]{2,1,0:T(8,128)(2,1)}), bf16[3,2048,256]{2,1,0:T(8,128)(2,1)}) %all-gather.3.cloned.1.call-update) | async-done | bytes 3145744 | tf_op jit(solution)/shard_map/all_gather | solution.py:44
  96.5 67.6 %all-gather.5.cloned.1.call-done = bf16[1024,2048]{1,0:T(8,128)(2,1)} async-done(((bf16[1024,256]{1,0:T(8,128)(2,1)}), bf16[1024,2048]{1,0:T(8,128)(2,1)}) %all-gather.5.cloned.1.call-update) | async-done | bytes 4194320 | tf_op jit(solution)/shard_map/all_gather | solution.py:40
  164.0 6.6 %fusion.7 = bf16[3,1024,256]{1,2,0:T(8,128)(2,1)S(1)} fusion(bf16[3,2048,256]{2,1,0:T(8,128)(2,1)} %all-gather.3.cloned.1.call-done, bf16[1024,2048]{1,0:T(8,128)(2,1)} %all-gather.5.cloned.1.call-done), kind=kOutput, calls=%fused_computation.16 | convolution fusion | flops 3222011904 | bytes 8912896 | tf_op jit(solution)/shard_map/tr,grc->gtc/dot_general | solution.py:41
  170.7 1.5 slice_convert_fusion.1
  172.2 1.3 copy.14
  173.5 2.1 fusion.31
  176.2 1.9 collective-permute-start
  178.6 7.2 %collective-permute-done = f32[264,128]{1,0:T(8,128)S(1)} collective-permute-done((f32[264,128]{1,0:T(8,128)S(1)}, f32[264,128]{1,0:T(8,128)S(1)}, u32[]{:S(2)}, u32[]{:S(2)}) %collective-permute-start) | collective-permute-done | bytes 135200 | tf_op jit(solution)/shard_map/ppermute | solution.py:12
  185.9 1.9 collective-permute-start.1
  189.2 6.3 %collective-permute-done.1 = f32[264,128]{1,0:T(8,128)S(1)} collective-permute-done((f32[264,128]{1,0:T(8,128)S(1)}, f32[264,128]{1,0:T(8,128)S(1)}, u32[]{:S(2)}, u32[]{:S(2)}) %collective-permute-start.1) | collective-permute-done | bytes 135200 | tf_op jit(solution)/shard_map/ppermute | solution.py:12
  197.4 1.9 collective-permute-start.2
  199.3 3.9 %fusion.13 = f32[512,2,128]{0,2,1:T(8,128)} fusion(bf16[1024,2,128]{0,2,1:T(8,128)(2,1)S(1)} %bitcast.50, bf16[512,2,128]{0,2,1:T(8,128)(2,1)} %bitcast.54, pred[512,1024]{1,0:T(8,128)(4,1)} %fusion.2, f32[1024,2,128]{2,0,1:T(8,128)} %copy.14), kind=kOutput, calls=%fused_computation.21 | convolution fusion | flops 540278784 | bytes 2883584 | tf_op jit(solution)/shard_map/hbs,she->bhe/dot_general | solution.py:73
  204.8 2.9 %collective-permute-done.2 = f32[264,128]{1,0:T(8,128)} collective-permute-done((f32[264,128]{1,0:T(8,128)S(1)}, f32[264,128]{1,0:T(8,128)}, u32[]{:S(2)}, u32[]{:S(2)}) %collective-permute-start.2) | collective-permute-done | bytes 135200 | tf_op jit(solution)/shard_map/ppermute | solution.py:12
  207.7 1.2 slice.108
  210.2 1.0 select_add_fusion.2
  211.2 1.9 collective-permute-start.3
  213.9 7.8 %collective-permute-done.3 = f32[264,128]{1,0:T(8,128)S(1)} collective-permute-done((f32[264,128]{1,0:T(8,128)S(1)}, f32[264,128]{1,0:T(8,128)S(1)}, u32[]{:S(2)}, u32[]{:S(2)}) %collective-permute-start.3) | collective-permute-done | bytes 135200 | tf_op jit(solution)/shard_map/ppermute | solution.py:12
  223.7 1.9 collective-permute-start.4
  225.6 2.6 %fusion.14 = f32[512,2,128]{0,2,1:T(8,128)} fusion(bf16[512,2,128]{0,2,1:T(8,128)(2,1)} %bitcast.52, bf16[512,2,128]{0,2,1:T(8,128)(2,1)} %bitcast.53, bf16[512,2,128]{0,2,1:T(8,128)(2,1)S(1)} %bitcast.51, pred[512,512]{1,0:T(8,128)(4,1)S(1)} %fusion.25), kind=kOutput, calls=%fused_computation.22 | convolution fusion | flops 269484032 | bytes 1572864 | tf_op jit(solution)/shard_map/hbs,she->bhe/dot_general | solution.py:73
  228.8 3.0 %collective-permute-done.4 = f32[264,128]{1,0:T(8,128)S(1)} collective-permute-done((f32[264,128]{1,0:T(8,128)S(1)}, f32[264,128]{1,0:T(8,128)S(1)}, u32[]{:S(2)}, u32[]{:S(2)}) %collective-permute-start.4) | collective-permute-done | bytes 135200 | tf_op jit(solution)/shard_map/ppermute | solution.py:12
  234.9 1.8 multiply_reduce_fusion
  236.9 1.0 copy.23
  (44 shorter events, 11.7 us)
Async XLA Ops:
  6.5 89.9 %all-gather.3.cloned.1.call-start = ((), (), s32[]{:S(2)}) async-start(), calls=%async_computation | async-start | bytes 3194880 | tf_op jit(solution)/shard_map/all_gather | solution.py:44
  7.3 156.8 %all-gather.5.cloned.1.call-start = ((), (), s32[]{:S(2)}) async-start(), calls=%async_computation.1 | async-start | bytes 4718592 | tf_op jit(solution)/shard_map/all_gather | solution.py:40
  170.7 1.5 copy-start
  173.5 4.7 %copy-start.1 = (bf16[3,1024,256]{1,2,0:T(8,128)(2,1)S(1)}, bf16[3,1024,256]{1,2,0:T(8,128)(2,1)}, u32[]{:S(2)}) copy-start(bf16[3,1024,256]{1,2,0:T(8,128)(2,1)} %copy-done) | copy-start | bytes 4718596
  176.2 9.7 %collective-permute-start = (f32[264,128]{1,0:T(8,128)S(1)}, f32[264,128]{1,0:T(8,128)S(1)}, u32[]{:S(2)}, u32[]{:S(2)}) collective-permute-start(f32[264,128]{1,0:T(8,128)S(1)} %concatenate.7), channel_id=1, source_target_pairs={{0,8},{8,16},{16,24},{24,32},{32,40},{40,48},{48,56},{56,64},{64,7... | collective-permute-start | bytes 405512 | tf_op jit(solution)/shard_map/ppermute | solution.py:12
  185.9 9.6 %collective-permute-start.1 = (f32[264,128]{1,0:T(8,128)S(1)}, f32[264,128]{1,0:T(8,128)S(1)}, u32[]{:S(2)}, u32[]{:S(2)}) collective-permute-start(f32[264,128]{1,0:T(8,128)S(1)} %collective-permute-done), channel_id=1, source_target_pairs={{0,8},{8,16},{16,24},{24,32},{32,40},{40,48},{48,56},{56,64},{64,7... | collective-permute-start | bytes 405512 | tf_op jit(solution)/shard_map/ppermute | solution.py:12
  197.4 10.3 %collective-permute-start.2 = (f32[264,128]{1,0:T(8,128)S(1)}, f32[264,128]{1,0:T(8,128)}, u32[]{:S(2)}, u32[]{:S(2)}) collective-permute-start(f32[264,128]{1,0:T(8,128)S(1)} %select_add_fusion.3), channel_id=1, source_target_pairs={{0,16},{8,24},{16,32},{24,40},{32,48},{40,56},{48,64},{56,72},{64,... | collective-permute-start | bytes 405512 | tf_op jit(solution)/shard_map/ppermute | solution.py:12
  203.9 9.2 %copy-start.2 = (f32[1024,256]{0,1:T(8,128)S(1)}, f32[1024,256]{0,1:T(8,128)}, u32[]{:S(2)}) copy-start(f32[1024,256]{0,1:T(8,128)} %get-tuple-element.6) | copy-start | bytes 3145732
  211.2 23.1 %copy-start.3 = (s32[1024]{0:T(1024)S(1)}, s32[1024]{0:T(1024)}, u32[]{:S(2)}) copy-start(s32[1024]{0:T(1024)} %param.7) | copy-start | bytes 12292
  211.2 10.5 %collective-permute-start.3 = (f32[264,128]{1,0:T(8,128)S(1)}, f32[264,128]{1,0:T(8,128)S(1)}, u32[]{:S(2)}, u32[]{:S(2)}) collective-permute-start(f32[264,128]{1,0:T(8,128)S(1)} %select_add_fusion.2), channel_id=1, source_target_pairs={{0,32},{8,40},{16,48},{24,56},{32,64},{40,72},{48,80},{56,88},{64,... | collective-permute-start | bytes 405512 | tf_op jit(solution)/shard_map/ppermute | solution.py:12
  223.7 8.1 %collective-permute-start.4 = (f32[264,128]{1,0:T(8,128)S(1)}, f32[264,128]{1,0:T(8,128)S(1)}, u32[]{:S(2)}, u32[]{:S(2)}) collective-permute-start(f32[264,128]{1,0:T(8,128)S(1)} %select_add_fusion.1), channel_id=1, source_target_pairs={{0,64},{8,72},{16,80},{24,88},{32,96},{40,104},{48,112},{56,120},{... | collective-permute-start | bytes 405512 | tf_op jit(solution)/shard_map/ppermute | solution.py:12
  233.6 3.2 %copy-start.4 = (f32[256]{0:T(256)S(1)}, f32[256]{0:T(256)}, u32[]{:S(2)}) copy-start(f32[256]{0:T(256)} %param.6) | copy-start | bytes 3076
Sparse Core Ops, SparseCore 0:
  10.8 85.6 all-gather.2
  98.5 65.5 all-gather.4
where the time goes:
time: 245 us
  waiting for transfers between devices  180 us (73%)
  between operations  18.7 us (8%)
  matrix products  17 us (7%)
  local copies, waits for them, and re-layouts  11.1 us (5%)
  starting transfers between devices  9.63 us (4%)
  other arithmetic  7.82 us (3%)
    all_gather x1, waiting for transfers between devices, per_device(): lax.all_gather(w_qkv, 'ctx', axis=1, tiled=True)  84.3 us
    all_gather x1, waiting for transfers between devices, per_device(): whole = lax.all_gather(tokens, 'head', axis=1, tiled=True)  67.6 us
    ppermute x5, waiting for transfers between devices, shifted(): lax.ppermute(value, axis, [(source, source + steps) for source in range(c...  27.2 us
    ppermute x5, starting transfers between devices, shifted(): lax.ppermute(value, axis, [(source, source + steps) for source in range(c...  9.59 us
    dot_general x1, matrix products, per_device(): jnp.einsum('tr,grc->gtc', whole, lax.all_gather(w_qkv, 'ctx', axis=1, til...  6.6 us
    dot_general x2, matrix products, per_device(): jnp.einsum('hbs,she->bhe', weights, values[:key_end], preferred_element_t...  6.48 us
    slice x8, local copies, waits for them, and re-layouts, state_scan(): linked = incoming[state_rows, 0] == running[state_rows, 0]  5.04 us
  transfers between devices with their start and end apart: 7, of which 7 were waited for; matrix products, arithmetic and copies ran while one was open for 6% of the time, Pallas kernels for 0%

commit v1 on v0

--- a/solution.py
+++ b/solution.py
@@ -37,7 +37,13 @@
 
 
 def per_device(tokens, w_qkv, out_gain, seg_ids):
-    whole = lax.all_gather(tokens, "head", axis=1, tiled=True)
+    count_2 = lax.axis_size("head")
+    held, parts = (tokens, [tokens])
+    for _ in range(count_2 - 1):
+        held = lax.ppermute(held, "head", [(i, (i + 1) % count_2) for i in range(count_2)])
+        parts.insert(0, held)
+    line = jnp.concatenate(parts, axis=1)
+    whole = jnp.roll(line, (lax.axis_index("head") + 1) * tokens.shape[1], axis=1)
     projected = jnp.einsum(
         "tr,grc->gtc",
         whole,

time: 245 us -> 215 us (0.88)
  waiting for transfers between devices: 180 us -> 115 us
  local copies, waits for them, and re-layouts: 11.1 us -> 31.2 us
  starting transfers between devices: 9.63 us -> 25.3 us
    ppermute x0 -> x7, waiting for transfers between devices: none -> 87.6 us  [per_device(): lax.ppermute(held, 'head', [(i, (i + 1) % count_2) for i in range(count_2)])]
    all_gather x1, waiting for transfers between devices: 84.3 us -> 0.01 us  [per_device(): lax.all_gather(w_qkv, 'ctx', axis=1, tiled=True)]
    all_gather x1 -> x0, waiting for transfers between devices: 67.6 us -> none  [per_device(): whole = lax.all_gather(tokens, 'head', axis=1, tiled=True)]
    unnamed x10 -> x23, local copies, waits for them, and re-layouts: 0.02 us -> 18.6 us
    ppermute x0 -> x7, starting transfers between devices: none -> 15.7 us  [per_device(): lax.ppermute(held, 'head', [(i, (i + 1) % count_2) for i in range(count_2)])]
  transfers between devices with their start and end apart: 7 -> 13, of which waited for: 7 -> 12; matrix products, arithmetic and copies ran while one was open for 6% -> 16% of each run, Pallas kernels for 0% -> 0%
where the time goes in v1:
time: 215 us; the launch traced here: 214 us
  waiting for transfers between devices  115 us (53%)
  local copies, waits for them, and re-layouts  31.2 us (15%)
  starting transfers between devices  25.3 us (12%)
  between operations  18.5 us (9%)
  matrix products  16.2 us (8%)
  other arithmetic  8.54 us (4%)
    ppermute x7, waiting for transfers between devices, per_device(): lax.ppermute(held, 'head', [(i, (i + 1) % count_2) for i in range(count_2)])  87.6 us
    ppermute x5, waiting for transfers between devices, shifted(): lax.ppermute(value, axis, [(source, source + steps) for source in range(c...  26.3 us
    unnamed x23, local copies, waits for them, and re-layouts  18.6 us
    ppermute x7, starting transfers between devices, per_device(): lax.ppermute(held, 'head', [(i, (i + 1) % count_2) for i in range(count_2)])  15.7 us
    ppermute x5, starting transfers between devices, shifted(): lax.ppermute(value, axis, [(source, source + steps) for source in range(c...  9.59 us
    dot_general x1, matrix products, per_device(): jnp.einsum('tr,grc->gtc', whole, lax.all_gather(w_qkv, 'ctx', axis=1, til...  6.63 us
    dot_general x2, matrix products, per_device(): jnp.einsum('hbs,she->bhe', weights, values[:key_end], preferred_element_t...  5.77 us
    slice x8, local copies, waits for them, and re-layouts, state_scan(): linked = incoming[state_rows, 0] == running[state_rows, 0]  4.8 us
  transfers between devices with their start and end apart: 13, of which 12 were waited for; matrix products, arithmetic and copies ran while one was open for 16% of the time, Pallas kernels for 0%

profile of v1, /device:TPU:32, one launch (start us, length us, event | category | flops | bytes accessed | tf_op | source)
XLA Modules:
  0.0 214.4 jit_solution(4647401746939299892)
XLA Ops:
  7.3 4.3 %collective-permute-start = (bf16[1024,256]{1,0:T(8,128)(2,1)}, bf16[1024,256]{1,0:T(8,128)(2,1)S(1)}, u32[]{:S(2)}, u32[]{:S(2)}) collective-permute-start(bf16[1024,256]{1,0:T(8,128)(2,1)} %param.4), channel_id=1, source_target_pairs={{0,1},{1,2},{2,3},{3,4},{4,5},{5,6},{6,7},{7,0},{8,9},{9,10},{10,1... | collective-permute-start | bytes 1572872 | tf_op jit(solution)/shard_map/ppermute | solution.py:43
  11.5 18.8 %collective-permute-done = bf16[1024,256]{1,0:T(8,128)(2,1)S(1)} collective-permute-done((bf16[1024,256]{1,0:T(8,128)(2,1)}, bf16[1024,256]{1,0:T(8,128)(2,1)S(1)}, u32[]{:S(2)}, u32[]{:S(2)}) %collective-permute-start) | collective-permute-done | bytes 524320 | tf_op jit(solution)/shard_map/ppermute | solution.py:43
  32.2 14.3 %collective-permute-done.1 = bf16[1024,256]{1,0:T(8,128)(2,1)S(1)} collective-permute-done((bf16[1024,256]{1,0:T(8,128)(2,1)S(1)}, bf16[1024,256]{1,0:T(8,128)(2,1)S(1)}, u32[]{:S(2)}, u32[]{:S(2)}) %collective-permute-start.1) | collective-permute-done | bytes 524320 | tf_op jit(solution)/shard_map/ppermute | solution.py:43
  48.5 13.4 %collective-permute-done.2 = bf16[1024,256]{1,0:T(8,128)(2,1)S(1)} collective-permute-done((bf16[1024,256]{1,0:T(8,128)(2,1)S(1)}, bf16[1024,256]{1,0:T(8,128)(2,1)S(1)}, u32[]{:S(2)}, u32[]{:S(2)}) %collective-permute-start.2) | collective-permute-done | bytes 524320 | tf_op jit(solution)/shard_map/ppermute | solution.py:43
  63.7 12.4 %collective-permute-done.3 = bf16[1024,256]{1,0:T(8,128)(2,1)S(1)} collective-permute-done((bf16[1024,256]{1,0:T(8,128)(2,1)S(1)}, bf16[1024,256]{1,0:T(8,128)(2,1)S(1)}, u32[]{:S(2)}, u32[]{:S(2)}) %collective-permute-start.3) | collective-permute-done | bytes 524320 | tf_op jit(solution)/shard_map/ppermute | solution.py:43
  78.1 11.5 %collective-permute-done.4 = bf16[1024,256]{1,0:T(8,128)(2,1)S(1)} collective-permute-done((bf16[1024,256]{1,0:T(8,128)(2,1)S(1)}, bf16[1024,256]{1,0:T(8,128)(2,1)S(1)}, u32[]{:S(2)}, u32[]{:S(2)}) %collective-permute-start.4) | collective-permute-done | bytes 524320 | tf_op jit(solution)/shard_map/ppermute | solution.py:43
  89.6 1.9 collective-permute-start.5
  94.2 8.1 %collective-permute-done.5 = bf16[1024,256]{1,0:T(8,128)(2,1)} collective-permute-done((bf16[1024,256]{1,0:T(8,128)(2,1)S(1)}, bf16[1024,256]{1,0:T(8,128)(2,1)}, u32[]{:S(2)}, u32[]{:S(2)}) %collective-permute-start.5) | collective-permute-done | bytes 524320 | tf_op jit(solution)/shard_map/ppermute | solution.py:43
  105.8 9.1 %collective-permute-done.6 = bf16[1024,256]{1,0:T(8,128)(2,1)} collective-permute-done((bf16[1024,256]{1,0:T(8,128)(2,1)}, bf16[1024,256]{1,0:T(8,128)(2,1)}, u32[]{:S(2)}, u32[]{:S(2)}) %collective-permute-start.6) | collective-permute-done | bytes 524320 | tf_op jit(solution)/shard_map/ppermute | solution.py:43
  114.9 1.9 constant_dynamic-update-slice_fusion.15
  116.8 1.9 constant_dynamic-update-slice_fusion.14
  124.1 1.9 constant_dynamic-update-slice_fusion.7
  126.0 1.9 constant_dynamic-update-slice_fusion.6
  133.3 6.6 %fusion.8 = bf16[3,1024,256]{1,2,0:T(8,128)(2,1)S(1)} fusion(bf16[3,2048,256]{2,1,0:T(8,128)(2,1)} %all-gather.2.cloned.1.call-done, bf16[1024,4096]{1,0:T(8,128)(2,1)} %constant_dynamic-update-slice_fusion, s32[]{:T(128)S(6)} %select_n.74), kind=kOutput, calls=%fused_computation.17 | convolution fusion | flops 3222011904 | bytes 8912900 | tf_op jit(solution)/shard_map/tr,grc->gtc/dot_general | solution.py:47
  143.5 2.1 fusion.32
  146.4 1.9 collective-permute-start.7
  149.8 6.2 %collective-permute-done.7 = f32[264,128]{1,0:T(8,128)S(1)} collective-permute-done((f32[264,128]{1,0:T(8,128)S(1)}, f32[264,128]{1,0:T(8,128)S(1)}, u32[]{:S(2)}, u32[]{:S(2)}) %collective-permute-start.7) | collective-permute-done | bytes 135200 | tf_op jit(solution)/shard_map/ppermute | solution.py:12
  159.1 6.5 %collective-permute-done.8 = f32[264,128]{1,0:T(8,128)S(1)} collective-permute-done((f32[264,128]{1,0:T(8,128)S(1)}, f32[264,128]{1,0:T(8,128)S(1)}, u32[]{:S(2)}, u32[]{:S(2)}) %collective-permute-start.8) | collective-permute-done | bytes 135200 | tf_op jit(solution)/shard_map/ppermute | solution.py:12
  167.5 1.9 collective-permute-start.9
  169.4 4.0 %fusion.14 = f32[512,2,128]{0,2,1:T(8,128)} fusion(bf16[1024,2,128]{0,2,1:T(8,128)(2,1)} %bitcast.50, bf16[512,2,128]{0,2,1:T(8,128)(2,1)S(1)} %bitcast.54, pred[512,1024]{1,0:T(8,128)(4,1)} %fusion.3, f32[1024,2,128]{2,0,1:T(8,128)} %copy.14), kind=kOutput, calls=%fused_computation.22 | convolution fusion | flops 540278784 | bytes 2883584 | tf_op jit(solution)/shard_map/hbs,she->bhe/dot_general | solution.py:79
  181.2 1.9 collective-permute-start.10
  183.9 7.8 %collective-permute-done.10 = f32[264,128]{1,0:T(8,128)S(1)} collective-permute-done((f32[264,128]{1,0:T(8,128)S(1)}, f32[264,128]{1,0:T(8,128)S(1)}, u32[]{:S(2)}, u32[]{:S(2)}) %collective-permute-start.10) | collective-permute-done | bytes 135200 | tf_op jit(solution)/shard_map/ppermute | solution.py:12
  193.6 1.9 collective-permute-start.11
  197.8 3.9 %collective-permute-done.11 = f32[264,128]{1,0:T(8,128)S(1)} collective-permute-done((f32[264,128]{1,0:T(8,128)S(1)}, f32[264,128]{1,0:T(8,128)S(1)}, u32[]{:S(2)}, u32[]{:S(2)}) %collective-permute-start.11) | collective-permute-done | bytes 135200 | tf_op jit(solution)/shard_map/ppermute | solution.py:12
  (69 shorter events, 49.6 us)
Async XLA Ops:
  6.5 116.7 %copy-start.1 = (bf16[1024,256]{1,0:T(8,128)(2,1)S(1)}, bf16[1024,256]{1,0:T(8,128)(2,1)}, u32[]{:S(2)}) copy-start(bf16[1024,256]{1,0:T(8,128)(2,1)} %param.4) | copy-start | bytes 1572868
  6.5 126.7 %all-gather.2.cloned.1.call-start = ((), (), s32[]{:S(2)}) async-start(), calls=%async_computation | async-start | bytes 3194880 | tf_op jit(solution)/shard_map/all_gather | solution.py:50
  7.3 23.1 %collective-permute-start = (bf16[1024,256]{1,0:T(8,128)(2,1)}, bf16[1024,256]{1,0:T(8,128)(2,1)S(1)}, u32[]{:S(2)}, u32[]{:S(2)}) collective-permute-start(bf16[1024,256]{1,0:T(8,128)(2,1)} %param.4), channel_id=1, source_target_pairs={{0,1},{1,2},{2,3},{3,4},{4,5},{5,6},{6,7},{7,0},{8,9},{9,10},{10,1... | collective-permute-start | bytes 1572872 | tf_op jit(solution)/shard_map/ppermute | solution.py:43
  30.3 16.2 %collective-permute-start.1 = (bf16[1024,256]{1,0:T(8,128)(2,1)S(1)}, bf16[1024,256]{1,0:T(8,128)(2,1)S(1)}, u32[]{:S(2)}, u32[]{:S(2)}) collective-permute-start(bf16[1024,256]{1,0:T(8,128)(2,1)S(1)} %collective-permute-done), channel_id=1, source_target_pairs={{0,1},{1,2},{2,3},{3,4},{4,5},{5,6},{6,7},{7,0},{8,9},{9,10},{10,1... | collective-permute-start | bytes 1572872 | tf_op jit(solution)/shard_map/ppermute | solution.py:43
  46.5 15.3 %collective-permute-start.2 = (bf16[1024,256]{1,0:T(8,128)(2,1)S(1)}, bf16[1024,256]{1,0:T(8,128)(2,1)S(1)}, u32[]{:S(2)}, u32[]{:S(2)}) collective-permute-start(bf16[1024,256]{1,0:T(8,128)(2,1)S(1)} %collective-permute-done.1), channel_id=1, source_target_pairs={{0,1},{1,2},{2,3},{3,4},{4,5},{5,6},{6,7},{7,0},{8,9},{9,10},{10,1... | collective-permute-start | bytes 1572872 | tf_op jit(solution)/shard_map/ppermute | solution.py:43
  61.8 14.4 %collective-permute-start.3 = (bf16[1024,256]{1,0:T(8,128)(2,1)S(1)}, bf16[1024,256]{1,0:T(8,128)(2,1)S(1)}, u32[]{:S(2)}, u32[]{:S(2)}) collective-permute-start(bf16[1024,256]{1,0:T(8,128)(2,1)S(1)} %collective-permute-done.2), channel_id=1, source_target_pairs={{0,1},{1,2},{2,3},{3,4},{4,5},{5,6},{6,7},{7,0},{8,9},{9,10},{10,1... | collective-permute-start | bytes 1572872 | tf_op jit(solution)/shard_map/ppermute | solution.py:43
  76.2 13.4 %collective-permute-start.4 = (bf16[1024,256]{1,0:T(8,128)(2,1)S(1)}, bf16[1024,256]{1,0:T(8,128)(2,1)S(1)}, u32[]{:S(2)}, u32[]{:S(2)}) collective-permute-start(bf16[1024,256]{1,0:T(8,128)(2,1)S(1)} %collective-permute-done.3), channel_id=1, source_target_pairs={{0,1},{1,2},{2,3},{3,4},{4,5},{5,6},{6,7},{7,0},{8,9},{9,10},{10,1... | collective-permute-start | bytes 1572872 | tf_op jit(solution)/shard_map/ppermute | solution.py:43
  89.6 12.7 %collective-permute-start.5 = (bf16[1024,256]{1,0:T(8,128)(2,1)S(1)}, bf16[1024,256]{1,0:T(8,128)(2,1)}, u32[]{:S(2)}, u32[]{:S(2)}) collective-permute-start(bf16[1024,256]{1,0:T(8,128)(2,1)S(1)} %collective-permute-done.4), channel_id=1, source_target_pairs={{0,1},{1,2},{2,3},{3,4},{4,5},{5,6},{6,7},{7,0},{8,9},{9,10},{10,1... | collective-permute-start | bytes 1572872 | tf_op jit(solution)/shard_map/ppermute | solution.py:43
  102.3 12.6 %collective-permute-start.6 = (bf16[1024,256]{1,0:T(8,128)(2,1)}, bf16[1024,256]{1,0:T(8,128)(2,1)}, u32[]{:S(2)}, u32[]{:S(2)}) collective-permute-start(bf16[1024,256]{1,0:T(8,128)(2,1)} %collective-permute-done.5), channel_id=1, source_target_pairs={{0,1},{1,2},{2,3},{3,4},{4,5},{5,6},{6,7},{7,0},{8,9},{9,10},{10,1... | collective-permute-start | bytes 1572872 | tf_op jit(solution)/shard_map/ppermute | solution.py:43
  139.9 1.2 copy-start
  145.6 58.4 %copy-start.2 = (s32[1024]{0:T(1024)S(1)}, s32[1024]{0:T(1024)}, u32[]{:S(2)}) copy-start(s32[1024]{0:T(1024)} %param.7) | copy-start | bytes 12292
  146.4 9.7 %collective-permute-start.7 = (f32[264,128]{1,0:T(8,128)S(1)}, f32[264,128]{1,0:T(8,128)S(1)}, u32[]{:S(2)}, u32[]{:S(2)}) collective-permute-start(f32[264,128]{1,0:T(8,128)S(1)} %concatenate.14), channel_id=1, source_target_pairs={{0,8},{8,16},{16,24},{24,32},{32,40},{40,48},{48,56},{56,64},{64,7... | collective-permute-start | bytes 405512 | tf_op jit(solution)/shard_map/ppermute | solution.py:12
  156.0 9.6 %collective-permute-start.8 = (f32[264,128]{1,0:T(8,128)S(1)}, f32[264,128]{1,0:T(8,128)S(1)}, u32[]{:S(2)}, u32[]{:S(2)}) collective-permute-start(f32[264,128]{1,0:T(8,128)S(1)} %collective-permute-done.7), channel_id=1, source_target_pairs={{0,8},{8,16},{16,24},{24,32},{32,40},{40,48},{48,56},{56,64},{64,7... | collective-permute-start | bytes 405512 | tf_op jit(solution)/shard_map/ppermute | solution.py:12
  167.5 10.3 %collective-permute-start.9 = (f32[264,128]{1,0:T(8,128)S(1)}, f32[264,128]{1,0:T(8,128)}, u32[]{:S(2)}, u32[]{:S(2)}) collective-permute-start(f32[264,128]{1,0:T(8,128)S(1)} %select_add_fusion.3), channel_id=1, source_target_pairs={{0,16},{8,24},{16,32},{24,40},{32,48},{40,56},{48,64},{56,72},{64,... | collective-permute-start | bytes 405512 | tf_op jit(solution)/shard_map/ppermute | solution.py:12
  169.4 37.0 %copy-start.3 = (f32[256]{0:T(256)S(1)}, f32[256]{0:T(256)}, u32[]{:S(2)}) copy-start(f32[256]{0:T(256)} %param.6) | copy-start | bytes 3076
  181.2 10.5 %collective-permute-start.10 = (f32[264,128]{1,0:T(8,128)S(1)}, f32[264,128]{1,0:T(8,128)S(1)}, u32[]{:S(2)}, u32[]{:S(2)}) collective-permute-start(f32[264,128]{1,0:T(8,128)S(1)} %select_add_fusion.2), channel_id=1, source_target_pairs={{0,32},{8,40},{16,48},{24,56},{32,64},{40,72},{48,80},{56,88},{64,... | collective-permute-start | bytes 405512 | tf_op jit(solution)/shard_map/ppermute | solution.py:12
  193.6 8.1 %collective-permute-start.11 = (f32[264,128]{1,0:T(8,128)S(1)}, f32[264,128]{1,0:T(8,128)S(1)}, u32[]{:S(2)}, u32[]{:S(2)}) collective-permute-start(f32[264,128]{1,0:T(8,128)S(1)} %select_add_fusion.1), channel_id=1, source_target_pairs={{0,64},{8,72},{16,80},{24,88},{32,96},{40,104},{48,112},{56,120},{... | collective-permute-start | bytes 405512 | tf_op jit(solution)/shard_map/ppermute | solution.py:12
Sparse Core Ops, SparseCore 0:
  10.8 85.6 all-gather.1
